TPU v7x, 256 devices: a whole 4x4x8 slice. The times are simulated.
256 devices in a mesh: scen: 64 (over y, x, z_hi, core), trade: 4 (over z_lo).
Axes of the slice: x: 4, y: 4, z: 8 (z_hi: 2, z_lo: 4; z = z_hi * 4 + z_lo), core: 2. Of those that a mesh axis runs over, the one named last changes fastest.
Arguments:
- payoffs: float32 [12, 12, 12, 4, 8192], P(None, None, None, 'trade', 'scen'), may hold values from -4 to 4
- sweep_counts: int32 [4, 8192], P('trade', 'scen'), may hold values from 1 to 6
- netting_map: int32 [4, 8192], P('trade'), may hold values from 0 to 511
- type_lengths: int32 [8], replicated, may hold values from 1 to 8192, 32768 in all
- type_diffusion: float32 [8], replicated, may hold values from 0.02 to 0.15
- type_discount: float32 [8], replicated, may hold values from 0.01 to 0.12
- factors: float32 [3, 8192], P(None, 'scen'), may hold values from -1 to 1
Outputs:
- exposures: float32 [8192, 512], P('scen', 'trade')
- allocation: float32 [4, 8192], P('trade', 'scen')
All inputs are finite; a program needn't handle non-finite values.
Results may differ from a plain program's by a relative error of at most 0.0055.
Values may be sent and summed in bfloat16 or wider, within the bound.
No kernel may reach another device: no remote copies, remote signals or barrier semaphores. Data moves between devices by JAX's collectives and lax.ppermute only.
A program may use at most 128 MiB of HBM per device.

v0:
```python
import jax
import jax.numpy as jnp
from jax import lax
from jax.sharding import PartitionSpec as P

GRID = 12
NETS = 512
TYPES = 8
MAX_SWEEPS = 6


def cheb_matrix():
    intervals = GRID - 1
    order_index = jnp.arange(GRID, dtype=jnp.float32)
    end_weights = jnp.where((order_index == 0) | (order_index == intervals), 0.5, 1.0).astype(
        jnp.float32
    )
    angles = jnp.pi * order_index[:, None] * order_index[None, :] / intervals
    return 2.0 / intervals * end_weights[:, None] * end_weights[None, :] * jnp.cos(angles)


def cheb_basis(factors):
    factor_basis = []
    for column in range(3):
        point = factors[column]
        recurrence = [jnp.ones_like(point), point]
        for degree in range(2, GRID):
            recurrence.append(2.0 * point * recurrence[-1] - recurrence[-2])
        factor_basis.append(jnp.stack(recurrence[:GRID], 0))
    product = factor_basis[0][:, None, None, :] * factor_basis[1][None, :, None, :]
    product = product * factor_basis[2][None, None, :, :]
    return product.reshape(GRID * GRID * GRID, -1).astype(jnp.bfloat16)


def price(grid_values, counts, trade_index, type_lengths, type_diffusion, type_discount):
    type_ends = jnp.cumsum(type_lengths)
    type_ids = jnp.sum((trade_index[:, None] >= type_ends[None, :]).astype(jnp.int32), axis=1)
    type_hot = (type_ids[:, None] == jnp.arange(TYPES, dtype=jnp.int32)[None, :]).astype(
        jnp.float32
    )
    diffusion = jnp.sum(type_hot * type_diffusion[None, :], axis=1)
    discount = jnp.sum(type_hot * type_discount[None, :], axis=1)

    def smooth_step(degree, field):
        padded = jnp.pad(field, ((1, 1), (1, 1), (1, 1), (0, 0)))
        beside = padded[2:, 1:-1, 1:-1] + padded[:-2, 1:-1, 1:-1]
        beside = beside + padded[1:-1, 2:, 1:-1] + padded[1:-1, :-2, 1:-1]
        beside = beside + padded[1:-1, 1:-1, 2:] + padded[1:-1, 1:-1, :-2]
        updated = field + diffusion * (beside - 6.0 * field) - discount * field
        return jnp.where(degree < counts, updated, field)

    field = lax.fori_loop(0, MAX_SWEEPS, smooth_step, grid_values)
    matrix = cheb_matrix()
    field = jnp.einsum("ai,ijlp->ajlp", matrix, field, precision=lax.Precision.HIGHEST)
    field = jnp.einsum("bj,ajlp->ablp", matrix, field, precision=lax.Precision.HIGHEST)
    field = jnp.einsum("cl,ablp->abcp", matrix, field, precision=lax.Precision.HIGHEST)
    return field.reshape(GRID * GRID * GRID, -1).astype(jnp.bfloat16)


def shards(
    payoffs, sweep_counts, netting_map, type_lengths, type_diffusion, type_discount, factors
):
    trades_here = payoffs.shape[4]
    scen_index = lax.axis_index("scen")
    group_index = lax.axis_index("trade")
    block_size = trades_here * lax.axis_size("scen")
    first_trade = group_index * block_size + scen_index * trades_here
    trade_index = first_trade + jnp.arange(trades_here, dtype=jnp.int32)
    coef_local = price(
        payoffs[:, :, :, 0, :],
        sweep_counts[0],
        trade_index,
        type_lengths,
        type_diffusion,
        type_discount,
    )
    group_ids = netting_map[0]
    classes = jnp.arange(NETS, dtype=jnp.int32)
    scen_rows = factors.shape[1]
    scen_total = scen_rows * lax.axis_size("scen")
    basis_rows = cheb_basis(factors)
    values = lax.dot_general(
        basis_rows,
        lax.all_gather(coef_local, "scen", axis=1, tiled=True),
        (((0,), (0,)), ((), ())),
        preferred_element_type=jnp.float32,
    )
    set_hot = (group_ids[:, None] == classes[None, :]).astype(jnp.float32)
    partial_value = jnp.dot(values, set_hot, precision=lax.Precision.HIGHEST)
    totals = lax.psum_scatter(partial_value, "trade", scatter_dimension=1, tiled=True)
    exposures = jnp.maximum(totals, 0.0)
    every_set = lax.all_gather(exposures, "trade", axis=1, tiled=True)
    weight_rows = jnp.dot(every_set, set_hot.T, precision=lax.Precision.HIGHEST)
    alloc_terms = jnp.sum(values * weight_rows, axis=0) / scen_total
    allocation = lax.psum_scatter(alloc_terms, "scen", scatter_dimension=0, tiled=True)
    return (exposures, allocation.reshape(1, trades_here))


def solution(mesh):
    return jax.shard_map(
        shards,
        mesh=mesh,
        in_specs=(
            P(None, None, None, "trade", "scen"),
            P("trade", "scen"),
            P("trade", None),
            P(),
            P(),
            P(),
            P(None, "scen"),
        ),
        out_specs=(P("scen", "trade"), P("trade", "scen")),
        check_vma=False,
    )
```

profile of v0, /device:TPU:2, one launch (start us, length us, event | category | flops | bytes accessed | tf_op | source)
XLA Modules:
  0.0 791.1 jit_solution(13713044818506615753)
XLA Ops:
  7.3 1.3 copy.21
  9.0 5.0 while.15
  9.1 0.7 fusion.45
  9.9 0.7 fusion.45
  10.8 0.7 fusion.45
  11.6 0.7 fusion.45
  12.5 0.7 fusion.45
  13.3 0.7 fusion.45
  14.0 1.6 fusion.19
  15.6 1.7 convolution_bitcast_fusion
  17.3 1.5 fusion.16
  18.8 0.9 convert_element_type.33
  19.7 0.2 reduce-scatter.2.cloned.1.call-start
  20.5 310.8 %all-gather.2.cloned.1.call-done = bf16[1728,8192]{1,0:T(8,128)(2,1)} async-done(((bf16[1728,128]{1,0:T(8,128)(2,1)}), bf16[1728,8192]{1,0:T(8,128)(2,1)}) %all-gather.2.cloned.1.call-update) | async-done | bytes 28311568 | tf_op jit(solution)/shard_map/all_gather | solution.py:84
  331.3 11.2 %fusion.39 = f32[128,8192]{1,0:T(8,128)S(1)} fusion(bf16[1728,128]{1,0:T(8,128)(2,1)S(1)} %convert_element_type.29, bf16[1728,8192]{1,0:T(8,128)(2,1)} %all-gather.2.cloned.1.call-done), kind=kOutput, calls=%fused_computation.97 | convolution fusion | flops 3623878656 | bytes 32948224 | tf_op jit(solution)/shard_map/dot_general | solution.py:82
  342.5 1.9 copy-done
  344.4 6.6 fusion.11
  351.0 0.6 dynamic-slice
  352.2 18.7 %reduce-scatter.2.cloned.1.call-done = f32[128,128]{1,0:T(8,128)} async-done(((f32[128,512]{1,0:T(8,128)}), f32[128,128]{1,0:T(8,128)}) %reduce-scatter.2.cloned.1.call-update) | async-done | bytes 65552 | tf_op jit(solution)/shard_map/reduce_scatter | solution.py:90
  371.0 0.8 broadcast_maximum_fusion
  371.8 14.0 %all_gather.7 = f32[128,512]{1,0:T(8,128)S(1)} all-gather(f32[128,128]{1,0:T(8,128)S(1)} %broadcast_maximum_fusion), channel_id=1, replica_groups=mesh['scen'=64,'trade'=4] {'trade'}, dimensions={1}, use_global_device_ids=true | all-gather | bytes 327680 | tf_op jit(solution)/shard_map/all_gather | solution.py:92
  385.8 11.0 %fusion.15 = f32[8192]{0:T(1024)S(1)} fusion(f32[128,8192]{1,0:T(8,128)} %copy-done, f32[128,512]{1,0:T(8,128)S(1)} %all_gather.7, s32[8192]{0:T(1024)S(1)} %bitcast.29), kind=kOutput, calls=%fused_computation.23 | convolution fusion | flops 6448734208 | bytes 4521984 | tf_op jit(solution)/shard_map/dot_general | solution.py:93
  396.9 386.8 %all-reduce.1 = f32[8192]{0:T(1024)S(1)} all-reduce(f32[8192]{0:T(1024)S(1)} %broadcast_multiply_fusion.1), channel_id=3, replica_groups=mesh['scen'=64,'trade'=4] {'scen'}, use_global_device_ids=true, to_apply=%region_8.9.clone | all-reduce | flops 8192 | bytes 65536
  783.7 0.6 dynamic-slice_bitcast_fusion
  (49 shorter events, 1.7 us)
Async XLA Ops:
  7.2 1.4 copy-start.6
  7.2 1.7 copy-start.4
  7.2 1.7 copy-start.3
  7.2 1.8 copy-start.7
  7.2 324.1 %all-gather.2.cloned.1.call-start = ((), (), s32[]{:S(2)}) async-start(), calls=%async_computation.1 | async-start | bytes 28753920 | tf_op jit(solution)/shard_map/all_gather | solution.py:84
  18.8 1.1 copy-start.2
  19.7 351.2 %reduce-scatter.2.cloned.1.call-start = ((), (), s32[]{:S(2)}) async-start(), calls=%async_computation.2 | async-start | bytes 327680 | tf_op jit(solution)/shard_map/reduce_scatter | solution.py:90
  20.5 323.9 %copy-start.5 = (s32[1,8192]{1,0:T(1,128)S(1)}, s32[1,8192]{1,0:T(1,128)}, u32[]{:S(2)}) copy-start(s32[1,8192]{1,0:T(1,128)} %param.11) | copy-start | bytes 98308
  342.5 1.9 copy-start
  344.4 6.6 copy-start.8
  371.8 25.0 %copy-start.1 = (f32[128,128]{1,0:T(8,128)}, f32[128,128]{1,0:T(8,128)S(1)}, u32[]{:S(2)}) copy-start(f32[128,128]{1,0:T(8,128)S(1)} %broadcast_maximum_fusion) | copy-start | bytes 196612
Sparse Core Ops, SparseCore 0:
  19.9 311.3 all-gather.1
  351.1 19.8 reduce-scatter.1
where the time goes:
time: 806 us; the launch traced here: 791 us
  blocking collectives  401 us (50%)
  waiting for transfers between devices  330 us (41%)
  matrix products  33.6 us (4%)
  between operations  14.9 us (2%)
    unnamed x1, blocking collectives  387 us
    all_gather x1, waiting for transfers between devices, shards(): lax.all_gather(coef_local, 'scen', axis=1, tiled=True)  311 us
    reduce_scatter x1, waiting for transfers between devices, shards(): lax.psum_scatter(partial_value, 'trade', scatter_dimension=1, tiled=True)  18.7 us
  transfers between devices with their start and end apart: 2, of which 2 were waited for; matrix products, arithmetic and copies ran while one was open for 0% of the time, Pallas kernels for 0%

commit v1 on v0

--- a/solution.py
+++ b/solution.py
@@ -74,25 +74,33 @@
         type_diffusion,
         type_discount,
     )
-    group_ids = netting_map[0]
-    classes = jnp.arange(NETS, dtype=jnp.int32)
-    scen_rows = factors.shape[1]
-    scen_total = scen_rows * lax.axis_size("scen")
-    basis_rows = cheb_basis(factors)
-    values = lax.dot_general(
+    own_sets = lax.dynamic_slice_in_dim(netting_map[0], scen_index * trades_here, trades_here)
+    coef_rows = lax.all_gather(coef_local, "trade", axis=1, tiled=True)
+    set_ids = lax.all_gather(own_sets, "trade", axis=0, tiled=True)
+    sets_here = NETS // lax.axis_size("trade")
+    classes = group_index * sets_here + jnp.arange(sets_here, dtype=jnp.int32)
+    set_hot = (set_ids[:, None] == classes[None, :]).astype(jnp.bfloat16)
+    set_part = jnp.dot(coef_rows, set_hot, preferred_element_type=jnp.float32)
+    set_coef = lax.psum(set_part, "scen")
+    basis_rows = cheb_basis(factors).astype(jnp.float32)
+    totals = lax.dot_general(
         basis_rows,
-        lax.all_gather(coef_local, "scen", axis=1, tiled=True),
+        set_coef,
         (((0,), (0,)), ((), ())),
-        preferred_element_type=jnp.float32,
+        precision=lax.Precision.HIGHEST,
     )
-    set_hot = (group_ids[:, None] == classes[None, :]).astype(jnp.float32)
-    partial_value = jnp.dot(values, set_hot, precision=lax.Precision.HIGHEST)
-    totals = lax.psum_scatter(partial_value, "trade", scatter_dimension=1, tiled=True)
     exposures = jnp.maximum(totals, 0.0)
-    every_set = lax.all_gather(exposures, "trade", axis=1, tiled=True)
-    weight_rows = jnp.dot(every_set, set_hot.T, precision=lax.Precision.HIGHEST)
-    alloc_terms = jnp.sum(values * weight_rows, axis=0) / scen_total
-    allocation = lax.psum_scatter(alloc_terms, "scen", scatter_dimension=0, tiled=True)
+    scen_total = factors.shape[1] * lax.axis_size("scen")
+    weight_part = jnp.dot(basis_rows, exposures, precision=lax.Precision.HIGHEST)
+    weights = lax.psum(weight_part, "scen") / scen_total
+    trade_weights = lax.dot_general(
+        coef_rows.astype(jnp.float32),
+        weights,
+        (((0,), (0,)), ((), ())),
+        precision=lax.Precision.HIGHEST,
+    )
+    alloc_terms = jnp.sum(trade_weights * set_hot.astype(jnp.float32), axis=1)
+    allocation = lax.psum_scatter(alloc_terms, "trade", scatter_dimension=0, tiled=True)
     return (exposures, allocation.reshape(1, trades_here))
 
 

time: 806 us -> 1640 us (2.03)
  waiting for transfers between devices: 330 us -> 1580 us
  blocking collectives: 401 us -> 21.4 us
  matrix products: 33.6 us -> 13.4 us
    psum x0 -> x2, waiting for transfers between devices: none -> 1540 us  [the longest x1 772 us: shards(): weights = lax.psum(weight_part, 'scen') / scen_total]
    unnamed x1, blocking collectives: 387 us -> 9.2 us
    all_gather x1, waiting for transfers between devices: 311 us -> 37.2 us  [shards(): coef_rows = lax.all_gather(coef_local, 'trade', axis=1, tiled=True)]
    dot_general x3 -> x4, matrix products: 28.8 us -> 8.61 us  [the longest x1 3.1 us: shards(): set_part = jnp.dot(coef_rows, set_hot, preferred_element_type=jnp.float32)]
    reduce_scatter x1 -> x0, waiting for transfers between devices: 18.7 us -> none  [shards(): lax.psum_scatter(partial_value, 'trade', scatter_dimension=1, tiled=True)]
  transfers between devices with their start and end apart: 2 -> 3, of which waited for: 2 -> 3; matrix products, arithmetic and copies ran while one was open for 0% -> 0% of each run, Pallas kernels for 0% -> 0%
where the time goes in v1:
time: 1640 us
  waiting for transfers between devices  1580 us (96%)
  blocking collectives  21.4 us (1%)
    psum x1, waiting for transfers between devices, shards(): weights = lax.psum(weight_part, 'scen') / scen_total  772 us
    psum x1, waiting for transfers between devices, shards(): set_coef = lax.psum(set_part, 'scen')  768 us
    all_gather x1, waiting for transfers between devices, shards(): coef_rows = lax.all_gather(coef_local, 'trade', axis=1, tiled=True)  37.2 us
  transfers between devices with their start and end apart: 3, of which 3 were waited for; matrix products, arithmetic and copies ran while one was open for 0% of the time, Pallas kernels for 0%

profile of v1, /device:TPU:2, one launch (start us, length us, event | category | flops | bytes accessed | tf_op | source)
XLA Modules:
  0.0 1636.8 jit_solution(8168996887689070114)
XLA Ops:
  7.3 0.8 reduce-window.8
  8.1 1.3 copy.21
  9.6 5.0 while.15
  9.8 0.7 fusion.49
  10.6 0.7 fusion.49
  11.4 0.7 fusion.49
  12.3 0.7 fusion.49
  13.1 0.7 fusion.49
  13.9 0.7 fusion.49
  14.6 1.6 fusion.13
  16.2 1.7 convolution_bitcast_fusion
  18.0 1.5 fusion.10
  19.5 0.9 convert_element_type.40
  20.5 12.2 all-gather
  32.7 37.2 %all-gather.3.cloned.1.call-done = bf16[1728,512]{1,0:T(8,128)(2,1)} async-done(((bf16[1728,128]{1,0:T(8,128)(2,1)}), bf16[1728,512]{1,0:T(8,128)(2,1)}) %all-gather.3.cloned.1.call-update) | async-done | bytes 1769488 | tf_op jit(solution)/shard_map/all_gather | solution.py:78
  69.9 3.1 fusion.18
  73.5 767.9 %all-reduce.5.cloned.1.call-done = f32[1728,128]{1,0:T(8,128)} async-done(((f32[1728,128]{1,0:T(8,128)}), f32[1728,128]{1,0:T(8,128)}) %all-reduce.5.cloned.1.call-update) | async-done | bytes 884752 | tf_op jit(solution)/shard_map/psum | solution.py:84
  841.4 1.8 convolution_maximum_fusion
  843.3 1.4 fusion.41
  844.8 0.6 dynamic-slice.1
  846.0 772.2 %all-reduce.7.cloned.1.call-done = f32[1728,128]{1,0:T(8,128)} async-done(((f32[1728,128]{1,0:T(8,128)}), f32[1728,128]{1,0:T(8,128)}) %all-reduce.7.cloned.1.call-update) | async-done | bytes 884752 | tf_op jit(solution)/shard_map/psum | solution.py:95
  1618.2 2.2 fusion.15
  1620.4 9.2 all-reduce.1
  1629.7 0.6 dynamic-slice_bitcast_fusion
  (51 shorter events, 1.7 us)
Async XLA Ops:
  7.2 13.3 copy-start
  7.2 2.3 copy-start.5
  7.2 2.3 copy-start.4
  7.2 2.4 copy-start.6
  7.2 62.7 %all-gather.3.cloned.1.call-start = ((), (), s32[]{:S(2)}) async-start(), calls=%async_computation | async-start | bytes 2211840 | tf_op jit(solution)/shard_map/all_gather | solution.py:78
  19.5 13.2 copy-start.3
  20.4 821.0 %all-reduce.5.cloned.1.call-start = ((), (), s32[]{:S(2)}) async-start(), calls=%async_computation.1 | async-start | bytes 1769472 | tf_op jit(solution)/shard_map/psum | solution.py:84
  73.0 1545.2 %all-reduce.7.cloned.1.call-start = ((), (), s32[]{:S(2)}) async-start(), calls=%async_computation.2 | async-start | bytes 1769472 | tf_op jit(solution)/shard_map/psum | solution.py:95
  843.3 777.2 %copy-start.2 = (f32[128,128]{1,0:T(8,128)}, f32[128,128]{1,0:T(8,128)S(1)}, u32[]{:S(2)}) copy-start(f32[128,128]{1,0:T(8,128)S(1)} %convolution_maximum_fusion) | copy-start | bytes 196612
  843.3 1.5 copy-start.7
  843.3 774.9 %copy-start.1 = (bf16[1728,512]{1,0:T(8,128)(2,1)S(1)}, bf16[1728,512]{1,0:T(8,128)(2,1)}, u32[]{:S(2)}) copy-start(bf16[1728,512]{1,0:T(8,128)(2,1)} %all-gather.3.cloned.1.call-done) | copy-start | bytes 5308420
Sparse Core Ops, SparseCore 0:
  20.5 49.3 all-gather.2
  73.2 768.2 all-reduce.4
  844.9 773.2 all-reduce.6

commit v2 on v1

--- a/solution.py
+++ b/solution.py
@@ -1,7 +1,7 @@
 import jax
 import jax.numpy as jnp
 from jax import lax
-from jax.sharding import PartitionSpec as P
+from jax.sharding import Mesh, PartitionSpec as P
 
 GRID = 12
 NETS = 512
@@ -57,13 +57,25 @@
     return field.reshape(GRID * GRID * GRID, -1).astype(jnp.bfloat16)
 
 
+SCEN_PARTS = (("y", 4), ("x", 4), ("zh", 2), ("core", 2))
+SCEN = tuple(name for name, _ in SCEN_PARTS)
+
+
+def scen_sum(part):
+    for name in reversed(SCEN):
+        part = lax.psum_scatter(part, name, scatter_dimension=0, tiled=True)
+    for name in SCEN:
+        part = lax.all_gather(part, name, axis=0, tiled=True)
+    return part
+
+
 def shards(
     payoffs, sweep_counts, netting_map, type_lengths, type_diffusion, type_discount, factors
 ):
     trades_here = payoffs.shape[4]
-    scen_index = lax.axis_index("scen")
+    scen_index = lax.axis_index(SCEN)
     group_index = lax.axis_index("trade")
-    block_size = trades_here * lax.axis_size("scen")
+    block_size = trades_here * lax.axis_size(SCEN)
     first_trade = group_index * block_size + scen_index * trades_here
     trade_index = first_trade + jnp.arange(trades_here, dtype=jnp.int32)
     coef_local = price(
@@ -81,7 +93,7 @@
     classes = group_index * sets_here + jnp.arange(sets_here, dtype=jnp.int32)
     set_hot = (set_ids[:, None] == classes[None, :]).astype(jnp.bfloat16)
     set_part = jnp.dot(coef_rows, set_hot, preferred_element_type=jnp.float32)
-    set_coef = lax.psum(set_part, "scen")
+    set_coef = scen_sum(set_part)
     basis_rows = cheb_basis(factors).astype(jnp.float32)
     totals = lax.dot_general(
         basis_rows,
@@ -90,9 +102,9 @@
         precision=lax.Precision.HIGHEST,
     )
     exposures = jnp.maximum(totals, 0.0)
-    scen_total = factors.shape[1] * lax.axis_size("scen")
+    scen_total = factors.shape[1] * lax.axis_size(SCEN)
     weight_part = jnp.dot(basis_rows, exposures, precision=lax.Precision.HIGHEST)
-    weights = lax.psum(weight_part, "scen") / scen_total
+    weights = scen_sum(weight_part) / scen_total
     trade_weights = lax.dot_general(
         coef_rows.astype(jnp.float32),
         weights,
@@ -105,18 +117,20 @@
 
 
 def solution(mesh):
+    parts = mesh.devices.reshape(tuple(size for _, size in SCEN_PARTS) + (mesh.shape["trade"],))
+    fine = Mesh(parts, SCEN + ("trade",))
     return jax.shard_map(
         shards,
-        mesh=mesh,
+        mesh=fine,
         in_specs=(
-            P(None, None, None, "trade", "scen"),
-            P("trade", "scen"),
+            P(None, None, None, "trade", SCEN),
+            P("trade", SCEN),
             P("trade", None),
             P(),
             P(),
             P(),
-            P(None, "scen"),
+            P(None, SCEN),
         ),
-        out_specs=(P("scen", "trade"), P("trade", "scen")),
+        out_specs=(P(SCEN, "trade"), P("trade", SCEN)),
         check_vma=False,
     )

time: 1640 us -> 323 us (0.20)
  waiting for transfers between devices: 1580 us -> 126 us
  blocking collectives: 21.4 us -> 147 us
    psum x2 -> x0, waiting for transfers between devices: 1540 us -> none  [the longest x1 772 us: shards(): weights = lax.psum(weight_part, 'scen') / scen_total]
    reduce_scatter x0 -> x4, waiting for transfers between devices: none -> 83 us  [scen_sum(): part = lax.psum_scatter(part, name, scatter_dimension=0, tiled=True)]
    all_gather x0 -> x8, blocking collectives: none -> 76.4 us  [scen_sum(): part = lax.all_gather(part, name, axis=0, tiled=True)]
    unnamed x1 -> x5, blocking collectives: 9.2 us -> 58.5 us
  transfers between devices with their start and end apart: 3 -> 9, of which waited for: 3 -> 8; matrix products, arithmetic and copies ran while one was open for 0% -> 1% of each run, Pallas kernels for 0% -> 0%
where the time goes in v2:
time: 323 us
  blocking collectives  147 us (46%)
  waiting for transfers between devices  126 us (39%)
  between operations  16.1 us (5%)
  matrix products  11.1 us (3%)
  starting transfers between devices  10.2 us (3%)
  local copies, waits for them, and re-layouts  6.35 us (2%)
  other arithmetic  5.29 us (2%)
    reduce_scatter x4, waiting for transfers between devices, scen_sum(): part = lax.psum_scatter(part, name, scatter_dimension=0, tiled=True)  83 us
    all_gather x8, blocking collectives, scen_sum(): part = lax.all_gather(part, name, axis=0, tiled=True)  76.4 us
    unnamed x5, blocking collectives  58.5 us
    all_gather x1, waiting for transfers between devices, shards(): coef_rows = lax.all_gather(coef_local, 'trade', axis=1, tiled=True)  37.3 us
    all_gather x1, blocking collectives, shards(): set_ids = lax.all_gather(own_sets, 'trade', axis=0, tiled=True)  12.2 us
    unnamed x4, starting transfers between devices  9.99 us
  transfers between devices with their start and end apart: 9, of which 8 were waited for; matrix products, arithmetic and copies ran while one was open for 1% of the time, Pallas kernels for 0%

profile of v2, /device:TPU:2, one launch (start us, length us, event | category | flops | bytes accessed | tf_op | source)
XLA Modules:
  0.0 322.6 jit_solution(538453586790692568)
XLA Ops:
  9.6 5.0 %while.15 = (s32[]{:T(128)}, f32[12,12,12,128]{3,2,1,0:T(8,128)S(1)}, s32[128]{0:T(128)S(1)}, f32[128]{0:T(128)S(1)}, f32[128]{0:T(128)S(1)}, /*index=5*/s32[]{:T(128)}) while((s32[]{:T(128)}, f32[12,12,12,128]{3,2,1,0:T(8,128)S(1)}, s32[128]{0:T(128)S(1)}, f32[128]{0:T(128)S(1)}, f32[128]{0:T(128)S(1)}, /*index=5*/s32[]{:T(128)}) %tuple.93), condition=%wide.region_5.6_spmd, body=%wide.region_4.5_spmd.sunk | while | flops 2654338 | bytes 3540817 | solution.py:52
  20.5 12.2 %all-gather = s32[1,512]{1,0:T(1,128)S(1)} all-gather(s32[1,128]{1,0:T(1,128)S(1)} %constant_dynamic-slice_fusion.2), channel_id=2, replica_groups=mesh['y'=4,'x'=4,'zh'=2,'core'=2,'trade'=4] {'trade'}, dimensions={1}, use_global_device_ids=true | all-gather | bytes 2560 | tf_op jit(solution)/shard_map/all_gather | solution.py:91
  32.6 37.3 %all-gather.7.cloned.1.call-done = bf16[1728,512]{1,0:T(8,128)(2,1)} async-done(((bf16[1728,128]{1,0:T(8,128)(2,1)}), bf16[1728,512]{1,0:T(8,128)(2,1)}) %all-gather.7.cloned.1.call-update) | async-done | bytes 1769488 | tf_op jit(solution)/shard_map/all_gather | solution.py:90
  69.9 3.1 fusion.22
  73.1 11.5 %reduce-scatter.13.cloned.1.call-done = f32[864,128]{1,0:T(8,128)} async-done(((f32[1728,128]{1,0:T(8,128)}), f32[864,128]{1,0:T(8,128)}) %reduce-scatter.13.cloned.1.call-update) | async-done | bytes 442384 | tf_op jit(solution)/shard_map/reduce_scatter | solution.py:66
  84.9 31.4 %reduce-scatter.15.cloned.1.call-done = f32[432,128]{1,0:T(8,128)} async-done(((f32[864,128]{1,0:T(8,128)}), f32[432,128]{1,0:T(8,128)}) %reduce-scatter.15.cloned.1.call-update) | async-done | bytes 221200 | tf_op jit(solution)/shard_map/reduce_scatter | solution.py:66
  116.2 13.0 %fusion = f32[112,128]{1,0:T(8,128)S(1)} fusion(f32[432,128]{1,0:T(8,128)} %reduce-scatter.15.cloned.1.call-done), kind=kCustom, calls=%all-reduce-scatter | all-reduce-scatter fusion | flops 57345 | bytes 279552
  135.0 11.8 %fusion.1 = f32[32,128]{1,0:T(8,128)S(1)} fusion(f32[108,128]{1,0:T(8,128)S(1)} %constant_dynamic-slice_fusion.1), kind=kCustom, calls=%all-reduce-scatter.1 | all-reduce-scatter fusion | flops 16385 | bytes 72704
  146.8 3.1 collective-permute-start.1
  151.6 11.9 %all-gather.1 = f32[4,27,128]{2,1,0:T(8,128)S(1)} all-gather(f32[1,27,128]{2,1,0:T(8,128)S(1)} %dynamic-slice_bitcast_fusion.1), channel_id=1, replica_groups=mesh['y'=4,'x'=4,'zh'=2,'core'=2,'trade'=4] {'y'}, dimensions={0}, use_global_device_ids=true | all-gather | bytes 69120 | tf_op jit(solution)/shard_map/all_gather | solution.py:68
  163.4 11.0 %all-gather.2 = f32[4,108,128]{2,1,0:T(8,128)S(1)} all-gather(f32[1,108,128]{2,1,0:T(8,128)S(1)} %reshape.91), channel_id=1, replica_groups=mesh['y'=4,'x'=4,'zh'=2,'core'=2,'trade'=4] {'x'}, dimensions={0}, use_global_device_ids=true | all-gather | bytes 276480 | tf_op jit(solution)/shard_map/all_gather | solution.py:68
  174.4 12.9 %all_gather.34 = f32[864,128]{1,0:T(8,128)S(1)} all-gather(f32[432,128]{1,0:T(8,128)S(1)} %reshape.92), channel_id=1, replica_groups=mesh['y'=4,'x'=4,'zh'=2,'core'=2,'trade'=4] {'zh'}, dimensions={0}, use_global_device_ids=true | all-gather | bytes 663552 | tf_op jit(solution)/shard_map/all_gather | solution.py:68
  187.3 2.4 all_gather.35
  191.9 8.6 %reduce-scatter.17.cloned.1.call-done = f32[864,128]{1,0:T(8,128)} async-done(((f32[1728,128]{1,0:T(8,128)}), f32[864,128]{1,0:T(8,128)}) %reduce-scatter.17.cloned.1.call-update) | async-done | bytes 442384 | tf_op jit(solution)/shard_map/reduce_scatter | solution.py:66
  200.6 31.5 %reduce-scatter.19.cloned.1.call-done = f32[432,128]{1,0:T(8,128)} async-done(((f32[864,128]{1,0:T(8,128)}), f32[432,128]{1,0:T(8,128)}) %reduce-scatter.19.cloned.1.call-update) | async-done | bytes 221200 | tf_op jit(solution)/shard_map/reduce_scatter | solution.py:66
  232.0 13.0 %fusion.2 = f32[112,128]{1,0:T(8,128)S(1)} fusion(f32[432,128]{1,0:T(8,128)} %reduce-scatter.19.cloned.1.call-done), kind=kCustom, calls=%all-reduce-scatter.2 | all-reduce-scatter fusion | flops 57345 | bytes 279552
  247.0 3.6 %collective-permute-done.2 = f32[12,128]{1,0:T(8,128)S(1)} collective-permute-done((f32[12,128]{1,0:T(8,128)S(1)}, f32[12,128]{1,0:T(8,128)S(1)}, u32[]{:S(2)}, u32[]{:S(2)}) %collective-permute-start.2) | collective-permute-done | bytes 6176
  250.8 11.8 %fusion.3 = f32[32,128]{1,0:T(8,128)S(1)} fusion(f32[108,128]{1,0:T(8,128)S(1)} %constant_dynamic-slice_fusion), kind=kCustom, calls=%all-reduce-scatter.3 | all-reduce-scatter fusion | flops 16385 | bytes 72704
  262.6 3.1 collective-permute-start.3
  267.2 11.9 %all-gather.3 = f32[4,27,128]{2,1,0:T(8,128)S(1)} all-gather(f32[1,27,128]{2,1,0:T(8,128)S(1)} %dynamic-slice_bitcast_fusion), channel_id=1, replica_groups=mesh['y'=4,'x'=4,'zh'=2,'core'=2,'trade'=4] {'y'}, dimensions={0}, use_global_device_ids=true | all-gather | bytes 69120 | tf_op jit(solution)/shard_map/all_gather | solution.py:68
  279.0 11.0 %all-gather.4 = f32[4,108,128]{2,1,0:T(8,128)S(1)} all-gather(f32[1,108,128]{2,1,0:T(8,128)S(1)} %reshape.95), channel_id=1, replica_groups=mesh['y'=4,'x'=4,'zh'=2,'core'=2,'trade'=4] {'x'}, dimensions={0}, use_global_device_ids=true | all-gather | bytes 276480 | tf_op jit(solution)/shard_map/all_gather | solution.py:68
  290.0 13.0 %all_gather.38 = f32[864,128]{1,0:T(8,128)S(1)} all-gather(f32[432,128]{1,0:T(8,128)S(1)} %reshape.96), channel_id=1, replica_groups=mesh['y'=4,'x'=4,'zh'=2,'core'=2,'trade'=4] {'zh'}, dimensions={0}, use_global_device_ids=true | all-gather | bytes 663552 | tf_op jit(solution)/shard_map/all_gather | solution.py:68
  303.0 2.4 all_gather.39
  306.6 9.0 %all-reduce.5 = f32[512]{0:T(512)S(1)} all-reduce(f32[512]{0:T(512)S(1)} %fusion.19), channel_id=11, replica_groups=mesh['y'=4,'x'=4,'zh'=2,'core'=2,'trade'=4] {'trade'}, use_global_device_ids=true, to_apply=%region_15.16.clone | all-reduce | flops 512 | bytes 4096
  (99 shorter events, 26.2 us)
Async XLA Ops:
  7.2 13.3 %copy-start = (s32[1,8192]{1,0:T(1,128)S(1)}, s32[1,8192]{1,0:T(1,128)}, u32[]{:S(2)}) copy-start(s32[1,8192]{1,0:T(1,128)} %param.11) | copy-start | bytes 98308
  7.2 2.3 copy-start.4
  7.2 2.3 copy-start.5
  7.2 2.4 copy-start.8
  7.2 62.7 %all-gather.7.cloned.1.call-start = ((), (), s32[]{:S(2)}) async-start(), calls=%async_computation.4 | async-start | bytes 2211840 | tf_op jit(solution)/shard_map/all_gather | solution.py:90
  20.4 64.2 %reduce-scatter.13.cloned.1.call-start = ((), (), s32[]{:S(2)}) async-start(), calls=%async_computation.5 | async-start | bytes 1327104 | tf_op jit(solution)/shard_map/reduce_scatter | solution.py:66
  73.0 11.6 %copy-start.3 = (f32[3,128]{1,0:T(4,128)S(1)}, f32[3,128]{1,0:T(4,128)}, u32[]{:S(2)}) copy-start(f32[3,128]{1,0:T(4,128)} %param.15) | copy-start | bytes 4612
  73.0 58.2 %copy-start.7 = (u32[256]{0:T(256)S(1)}, u32[256]{0:T(256)}, u32[]{:S(2)}) copy-start(u32[256]{0:T(256)} %constant.107) | copy-start | bytes 3076
  73.0 77.0 %copy-start.6 = (u32[256]{0:T(256)S(1)}, u32[256]{0:T(256)}, u32[]{:S(2)}) copy-start(u32[256]{0:T(256)} %constant.111) | copy-start | bytes 3076
  73.1 43.2 %reduce-scatter.15.cloned.1.call-start = ((), (), s32[]{:S(2)}) async-start(), calls=%async_computation.6 | async-start | bytes 663552 | tf_op jit(solution)/shard_map/reduce_scatter | solution.py:66
  84.6 115.9 %reduce-scatter.17.cloned.1.call-start = ((), (), s32[]{:S(2)}) async-start(), calls=%async_computation.7 | async-start | bytes 1327104 | tf_op jit(solution)/shard_map/reduce_scatter | solution.py:66
  129.2 5.5 %collective-permute-start = (f32[12,128]{1,0:T(8,128)S(1)}, f32[12,128]{1,0:T(8,128)S(1)}, u32[]{:S(2)}, u32[]{:S(2)}) collective-permute-start(f32[12,128]{1,0:T(8,128)S(1)} %slice.72), channel_id=1, source_target_pairs={{0,16},{16,32},{32,48},{1,17},{17,33},{33,49},{2,18},{18,34},{34,5... | collective-permute-start | bytes 18440
  146.8 4.6 %collective-permute-start.1 = (f32[15,128]{1,0:T(8,128)S(1)}, f32[15,128]{1,0:T(8,128)S(1)}, u32[]{:S(2)}, u32[]{:S(2)}) collective-permute-start(f32[15,128]{1,0:T(8,128)S(1)} %slice.73), channel_id=1, source_target_pairs={{0,64},{64,128},{128,192},{1,65},{65,129},{129,193},{2,66},{66,130... | collective-permute-start | bytes 23048
  190.4 10.2 %copy-start.2 = (f32[128,128]{1,0:T(8,128)}, f32[128,128]{1,0:T(8,128)S(1)}, u32[]{:S(2)}) copy-start(f32[128,128]{1,0:T(8,128)S(1)} %convolution_maximum_fusion) | copy-start | bytes 196612
  191.8 73.9 %copy-start.9 = (u32[256]{0:T(256)S(1)}, u32[256]{0:T(256)}, u32[]{:S(2)}) copy-start(u32[256]{0:T(256)} %constant.123) | copy-start | bytes 3076
  191.9 40.2 %reduce-scatter.19.cloned.1.call-start = ((), (), s32[]{:S(2)}) async-start(), calls=%async_computation.8 | async-start | bytes 663552 | tf_op jit(solution)/shard_map/reduce_scatter | solution.py:66
  245.0 5.5 %collective-permute-start.2 = (f32[12,128]{1,0:T(8,128)S(1)}, f32[12,128]{1,0:T(8,128)S(1)}, u32[]{:S(2)}, u32[]{:S(2)}) collective-permute-start(f32[12,128]{1,0:T(8,128)S(1)} %slice.74), channel_id=1, source_target_pairs={{0,16},{16,32},{32,48},{1,17},{17,33},{33,49},{2,18},{18,34},{34,5... | collective-permute-start | bytes 18440
  262.6 4.4 %collective-permute-start.3 = (f32[15,128]{1,0:T(8,128)S(1)}, f32[15,128]{1,0:T(8,128)S(1)}, u32[]{:S(2)}, u32[]{:S(2)}) collective-permute-start(f32[15,128]{1,0:T(8,128)S(1)} %slice.75), channel_id=1, source_target_pairs={{0,64},{64,128},{128,192},{1,65},{65,129},{129,193},{2,66},{66,130... | collective-permute-start | bytes 23048
  290.0 15.4 %copy-start.1 = (bf16[1728,512]{1,0:T(8,128)(2,1)S(1)}, bf16[1728,512]{1,0:T(8,128)(2,1)}, u32[]{:S(2)}) copy-start(bf16[1728,512]{1,0:T(8,128)(2,1)} %all-gather.7.cloned.1.call-done) | copy-start | bytes 5308420
Sparse Core Ops, SparseCore 0:
  20.5 49.3 all-gather.6
  73.2 11.3 reduce-scatter.12
  87.1 29.0 reduce-scatter.14
  192.0 8.4 reduce-scatter.16
  202.9 29.0 reduce-scatter.18
